TPU v7x, 32 devices: a whole 2x2x4 slice. The times are simulated.
32 devices in a mesh: tm: 8 (over y, x, core), row: 4 (over z).
Axes of the slice: x: 2, y: 2, z: 4, core: 2. Of those that a mesh axis runs over, the one named last changes fastest.
Arguments:
- section_maps: float32 [8, 1024, 1024], P('tm', 'row'), may hold values from -0.04375 to 1.09375, as said below
- terminal_cost: float32 [512, 512], P('row'), may hold values from -0.075 to 1.075, as said below
- terminal_states: float32 [512, 2048], replicated, may hold values from -6 to 6
Outputs:
- trajectories: float32 [8, 1024, 2048], P('tm', 'row')
- section_cost: float32 [8, 2048], P('tm', 'row')
Inputs may be any that keep to these rules, and one draw needn't show every extreme that they name: `section_maps`: each section map is its diagonal plus small entries off the diagonal. `terminal_cost`: symmetric.
All inputs are finite; a program needn't handle non-finite values.
Results may differ from a plain program's by a relative error of at most 0.0003.
Values sent between devices are 32-bit elements; how exact they have to be, the bound alone decides.
No kernel may reach another device: no remote copies, remote signals or barrier semaphores. Data moves between devices by JAX's collectives and lax.ppermute only.
A program may use at most 64 MiB of HBM per device.

v0:
```python
import jax
import jax.numpy as jnp
from jax import lax
from jax.sharding import PartitionSpec as P


def shifted(block, axis, distance):
    devices = range(lax.axis_size(axis))
    route = [(i - distance, i) for i in devices if i - distance in devices]
    return lax.ppermute(block, axis, route)


def product(left, right):
    return jnp.dot(left, right, precision=lax.Precision.HIGHEST, preferred_element_type=jnp.float32)


def body(section_maps, terminal_cost, terminal_states):
    running = section_maps[0]
    state_dim = running.shape[1] // 2
    tm_count = lax.axis_size("tm")
    tm_place = lax.axis_index("tm")
    for level_index in range((tm_count - 1).bit_length()):
        stride = 1 << level_index
        gathered = lax.all_gather(running, "row", axis=0, tiled=True)
        further = shifted(gathered, "tm", -stride)
        combined = product(running, further)
        running = jnp.where(tm_place + stride < tm_count, combined, running)
    portion = lax.all_gather(terminal_cost, "row", axis=0, tiled=True)
    columns = lax.dynamic_slice_in_dim(running, state_dim, portion.shape[0], 1)
    value_rows = running[:, :state_dim] + product(columns, portion)
    rows_traj = product(value_rows, terminal_states)
    regrouped = lax.all_to_all(rows_traj, "row", split_axis=1, concat_axis=0, tiled=True)
    section_cost = jnp.sum(regrouped[:state_dim] * regrouped[state_dim:], axis=0) / state_dim
    return (rows_traj[None], section_cost[None])


def solution(mesh):
    in_specs = (P("tm", "row", None), P("row", None), P())
    out_specs = (P("tm", "row", None), P("tm", "row"))
    return jax.shard_map(body, mesh=mesh, in_specs=in_specs, out_specs=out_specs, check_vma=False)
```

profile of v0, /device:TPU:0, one launch (start us, length us, event | category | flops | bytes accessed | tf_op | source)
XLA Modules:
  0.0 577.2 jit_solution(18376967483935607676)
XLA Ops:
  7.2 0.0 all-gather.12.cloned.1.call-start
  7.2 0.7 all-gather.12.cloned.1.call-update
  7.9 0.0 all-gather.6.cloned.1.call-start
  7.9 85.1 %all-gather.12.cloned.1.call-done = f32[1,1024,1024]{2,1,0:T(8,128)} async-done(((f32[1,256,1024]{2,1,0:T(8,128)}), f32[1,1024,1024]{2,1,0:T(8,128)}) %all-gather.12.cloned.1.call-update) | async-done | bytes 4194320 | tf_op jit(solution)/shard_map/all_gather | solution.py:24
  93.0 1.3 collective-permute-start
  94.3 8.1 %collective-permute-done = f32[1024,1024]{1,0:T(8,128)} collective-permute-done((f32[1024,1024]{1,0:T(8,128)}, f32[1024,1024]{1,0:T(8,128)}, u32[]{:S(2)}, u32[]{:S(2)}) %collective-permute-start) | collective-permute-done | bytes 4194336 | tf_op jit(solution)/shard_map/ppermute | solution.py:10
  102.4 7.4 %convolution_select_fusion.2 = f32[256,1024]{1,0:T(8,128)} fusion(f32[1024,1024]{1,0:T(8,128)} %collective-permute-done, f32[1,256,1024]{2,1,0:T(8,128)} %param.3, pred[]{:T(512)S(6)} %lt.11), kind=kOutput, calls=%fused_computation.3 | convolution fusion | flops 3221487616 | bytes 6291457 | tf_op jit(solution)/shard_map/dot_general | solution.py:14
  109.9 0.0 all-gather.8.cloned.1.call-start
  109.9 119.6 %all-gather.6.cloned.1.call-done = f32[1024,1024]{1,0:T(8,128)} async-done(((f32[256,1024]{1,0:T(8,128)}), f32[1024,1024]{1,0:T(8,128)}) %all-gather.6.cloned.1.call-update) | async-done | bytes 4194320 | tf_op jit(solution)/shard_map/all_gather | solution.py:24
  229.5 1.3 collective-permute-start.1
  230.8 93.1 %collective-permute-done.1 = f32[1024,1024]{1,0:T(8,128)} collective-permute-done((f32[1024,1024]{1,0:T(8,128)}, f32[1024,1024]{1,0:T(8,128)}, u32[]{:S(2)}, u32[]{:S(2)}) %collective-permute-start.1) | collective-permute-done | bytes 4194336 | tf_op jit(solution)/shard_map/ppermute | solution.py:10
  323.9 7.5 %convolution_select_fusion.1 = f32[256,1024]{1,0:T(8,128)} fusion(f32[256,1024]{1,0:T(8,128)} %convolution_select_fusion.2, f32[1024,1024]{1,0:T(8,128)} %collective-permute-done.1, pred[]{:T(512)S(6)} %lt.10), kind=kOutput, calls=%fused_computation.2 | convolution fusion | flops 3221487616 | bytes 6291457 | tf_op jit(solution)/shard_map/dot_general | solution.py:14
  331.5 0.0 all-gather.10.cloned.1.call-start
  331.5 79.5 %all-gather.8.cloned.1.call-done = f32[1024,1024]{1,0:T(8,128)} async-done(((f32[256,1024]{1,0:T(8,128)}), f32[1024,1024]{1,0:T(8,128)}) %all-gather.8.cloned.1.call-update) | async-done | bytes 4194320 | tf_op jit(solution)/shard_map/all_gather | solution.py:24
  411.0 1.5 collective-permute-start.2
  412.5 92.9 %collective-permute-done.2 = f32[1024,1024]{1,0:T(8,128)} collective-permute-done((f32[1024,1024]{1,0:T(8,128)}, f32[1024,1024]{1,0:T(8,128)}, u32[]{:S(2)}, u32[]{:S(2)}) %collective-permute-start.2) | collective-permute-done | bytes 4194336 | tf_op jit(solution)/shard_map/ppermute | solution.py:10
  505.4 6.6 %convolution_select_fusion = f32[256,1024]{1,0:T(8,128)S(1)} fusion(f32[256,1024]{1,0:T(8,128)} %convolution_select_fusion.1, f32[1024,1024]{1,0:T(8,128)} %collective-permute-done.2, pred[]{:T(512)S(6)} %lt.9), kind=kOutput, calls=%fused_computation.1 | convolution fusion | flops 3221487616 | bytes 6291457 | tf_op jit(solution)/shard_map/dot_general | solution.py:14
  512.0 0.0 all-gather.10.cloned.1.call-done
  512.0 2.3 fusion.2
  514.3 5.5 fusion.4
  519.8 0.2 copy.8
  520.0 50.0 %all_to_all.16 = f32[256,4,512]{2,0,1:T(8,128)S(1)} all-to-all(f32[256,4,512]{2,0,1:T(8,128)S(1)} %bitcast.21), channel_id=1, replica_groups=mesh['tm'=8,'row'=4] {'row'}, dimensions={1} | all-to-all | bytes 4194304 | tf_op jit(solution)/shard_map/all_to_all | solution.py:32
  570.0 0.1 fusion
  570.1 0.6 broadcast_multiply_fusion
  (5 shorter events, 0.1 us)
Async XLA Ops:
  7.2 85.9 %all-gather.12.cloned.1.call-start = ((), (), s32[]{:S(2)}) async-start(), calls=%async_computation.4 | async-start | bytes 5242880 | tf_op jit(solution)/shard_map/all_gather | solution.py:24
  7.9 221.6 %all-gather.6.cloned.1.call-start = ((), (), s32[]{:S(2)}) async-start(), calls=%async_computation.1 | async-start | bytes 5242880 | tf_op jit(solution)/shard_map/all_gather | solution.py:24
  93.0 9.4 %collective-permute-start = (f32[1024,1024]{1,0:T(8,128)}, f32[1024,1024]{1,0:T(8,128)}, u32[]{:S(2)}, u32[]{:S(2)}) collective-permute-start(f32[1024,1024]{1,0:T(8,128)} %bitcast.23), channel_id=1, source_target_pairs={{4,0},{8,4},{12,8},{16,12},{20,16},{24,20},{28,24},{5,1},{9,5},{13... | collective-permute-start | bytes 12582920 | tf_op jit(solution)/shard_map/ppermute | solution.py:10
  109.9 301.2 %all-gather.8.cloned.1.call-start = ((), (), s32[]{:S(2)}) async-start(), calls=%async_computation.2 | async-start | bytes 5242880 | tf_op jit(solution)/shard_map/all_gather | solution.py:24
  229.5 94.4 %collective-permute-start.1 = (f32[1024,1024]{1,0:T(8,128)}, f32[1024,1024]{1,0:T(8,128)}, u32[]{:S(2)}, u32[]{:S(2)}) collective-permute-start(f32[1024,1024]{1,0:T(8,128)} %all-gather.6.cloned.1.call-done), channel_id=1, source_target_pairs={{8,0},{12,4},{16,8},{20,12},{24,16},{28,20},{9,1},{13,5},{17,9},{2... | collective-permute-start | bytes 12582920 | tf_op jit(solution)/shard_map/ppermute | solution.py:10
  331.5 180.6 %all-gather.10.cloned.1.call-start = ((), (), s32[]{:S(2)}) async-start(), calls=%async_computation.3 | async-start | bytes 1310720 | tf_op jit(solution)/shard_map/all_gather | solution.py:28
  411.0 94.4 %collective-permute-start.2 = (f32[1024,1024]{1,0:T(8,128)}, f32[1024,1024]{1,0:T(8,128)}, u32[]{:S(2)}, u32[]{:S(2)}) collective-permute-start(f32[1024,1024]{1,0:T(8,128)} %all-gather.8.cloned.1.call-done), channel_id=1, source_target_pairs={{16,0},{20,4},{24,8},{28,12},{17,1},{21,5},{25,9},{29,13},{18,2},{... | collective-permute-start | bytes 12582920 | tf_op jit(solution)/shard_map/ppermute | solution.py:10
  519.8 50.2 %copy-start = (f32[256,2048]{1,0:T(8,128)}, f32[256,2048]{1,0:T(8,128)S(1)}, u32[]{:S(2)}) copy-start(f32[256,2048]{1,0:T(8,128)S(1)} %fusion.4) | copy-start | bytes 6291460
Sparse Core Ops, SparseCore 0:
  9.5 83.4 all-gather.11
  110.0 119.4 all-gather.5
  331.6 79.3 all-gather.7
  412.7 29.3 all-gather.9
where the time goes:
time: 577 us
  waiting for transfers between devices  479 us (83%)
  blocking collectives  50 us (9%)
  matrix products  29.3 us (5%)
  between operations  13.9 us (2%)
    all_gather x3, waiting for transfers between devices, body(): gathered = lax.all_gather(running, 'row', axis=0, tiled=True)  284 us
    ppermute x3, waiting for transfers between devices, shifted(): return lax.ppermute(block, axis, route)  194 us
    all_to_all x1, blocking collectives, body(): lax.all_to_all(rows_traj, 'row', split_axis=1, concat_axis=0, tiled=True)  50 us
    dot_general x5, matrix products, product(): jnp.dot(left, right, precision=lax.Precision.HIGHEST, preferred_element_t...  29.3 us
  transfers between devices with their start and end apart: 7, of which 6 were waited for; matrix products, arithmetic and copies ran while one was open for 1% of the time, Pallas kernels for 0%

commit v1 on v0

--- a/solution.py
+++ b/solution.py
@@ -2,6 +2,12 @@
 import jax.numpy as jnp
 from jax import lax
 from jax.sharding import PartitionSpec as P
+
+
+def state_strips_all(here_x, at_axis):
+    z2 = list(here_x.shape[1:])
+    z2[at_axis] *= here_x.shape[0]
+    return jnp.moveaxis(here_x, 0, at_axis).reshape(z2)
 
 
 def shifted(block, axis, distance):
@@ -21,7 +27,25 @@
     tm_place = lax.axis_index("tm")
     for level_index in range((tm_count - 1).bit_length()):
         stride = 1 << level_index
-        gathered = lax.all_gather(running, "row", axis=0, tiled=True)
+        lanes = lax.axis_size("row")
+        inbox = tuple(((dev_j, (dev_j + 1) % lanes) for dev_j in range(lanes)))
+        buffer = tuple(((num, no) for no, num in inbox))
+        long_array, tall = ([], [])
+        for ii in tuple(range(lanes - 1)):
+            if ii % 2 == 0:
+                long_array.append(
+                    lax.ppermute(
+                        long_array[-1] if long_array else running, axis_name="row", perm=inbox
+                    )
+                )
+            else:
+                tall.append(
+                    lax.ppermute(tall[-1] if tall else running, perm=buffer, axis_name="row")
+                )
+        left_arr = jnp.stack([*long_array[::-1], running, *tall], 0)
+        item_now = lax.axis_index("row") - len(long_array)
+        left_arr = left_arr[(jnp.arange(lanes) - item_now) % lanes]
+        gathered = state_strips_all(left_arr, 0)
         further = shifted(gathered, "tm", -stride)
         combined = product(running, further)
         running = jnp.where(tm_place + stride < tm_count, combined, running)

time: 577 us -> 595 us (1.031)
  waiting for transfers between devices: 479 us -> 438 us
  local copies, waits for them, and re-layouts: 0.21 us -> 33 us
  starting transfers between devices: 4.18 us -> 17 us
  other arithmetic: 0.73 us -> 8.72 us
    all_gather x3 -> x0, waiting for transfers between devices: 284 us -> none  [body(): gathered = lax.all_gather(running, 'row', axis=0, tiled=True)]
    ppermute x0 -> x9, waiting for transfers between devices: none -> 171 us  [the longest x6 121 us: body(): lax.ppermute(long_array[-1] if long_array else running, axis_name='row',...]
    ppermute x3, waiting for transfers between devices: 194 us -> 266 us  [shifted(): return lax.ppermute(block, axis, route)]
    gather x0 -> x6, local copies, waits for them, and re-layouts: none -> 31.2 us  [body(): left_arr = left_arr[(jnp.arange(lanes) - item_now) % lanes]]
    ppermute x0 -> x9, starting transfers between devices: none -> 12.9 us  [the longest x3 9.71 us: body(): lax.ppermute(tall[-1] if tall else running, perm=buffer, axis_name='row')]
    another operation x0 -> x3, other arithmetic: none -> 7.96 us  [body(): left_arr = jnp.stack([*long_array[::-1], running, *tall], 0)]
  transfers between devices with their start and end apart: 7 -> 13, of which waited for: 6 -> 12; matrix products, arithmetic and copies ran while one was open for 1% -> 1% of each run, Pallas kernels for 0% -> 0%
where the time goes in v1:
time: 595 us; the launch traced here: 594 us
  waiting for transfers between devices  438 us (74%)
  blocking collectives  49.7 us (8%)
  matrix products  34 us (6%)
  local copies, waits for them, and re-layouts  33 us (6%)
  starting transfers between devices  17 us (3%)
  between operations  14.2 us (2%)
  other arithmetic  8.72 us (1%)
    ppermute x3, waiting for transfers between devices, shifted(): return lax.ppermute(block, axis, route)  266 us
    ppermute x6, waiting for transfers between devices, body(): lax.ppermute(long_array[-1] if long_array else running, axis_name='row',...  121 us
    ppermute x3, waiting for transfers between devices, body(): lax.ppermute(tall[-1] if tall else running, perm=buffer, axis_name='row')  50.4 us
    all_to_all x1, blocking collectives, body(): lax.all_to_all(rows_traj, 'row', split_axis=1, concat_axis=0, tiled=True)  49.7 us
    dot_general x5, matrix products, product(): jnp.dot(left, right, precision=lax.Precision.HIGHEST, preferred_element_t...  34 us
    gather x6, local copies, waits for them, and re-layouts, body(): left_arr = left_arr[(jnp.arange(lanes) - item_now) % lanes]  31.2 us
  transfers between devices with their start and end apart: 13, of which 12 were waited for; matrix products, arithmetic and copies ran while one was open for 1% of the time, Pallas kernels for 0%

profile of v1, /device:TPU:0, one launch (start us, length us, event | category | flops | bytes accessed | tf_op | source)
XLA Modules:
  0.0 594.1 jit_solution(13641047911348865043)
XLA Ops:
  14.0 24.0 %collective-permute-done = f32[256,1024]{0,1:T(8,128)S(1)} collective-permute-done((f32[256,1024]{0,1:T(8,128)S(1)}, f32[256,1024]{0,1:T(8,128)S(1)}, u32[]{:S(2)}, u32[]{:S(2)}) %collective-permute-start) | collective-permute-done | bytes 1048608 | tf_op jit(solution)/shard_map/ppermute | solution.py:37
  38.0 21.2 %collective-permute-done.2 = f32[256,1024]{0,1:T(8,128)S(1)} collective-permute-done((f32[256,1024]{0,1:T(8,128)S(1)}, f32[256,1024]{0,1:T(8,128)S(1)}, u32[]{:S(2)}, u32[]{:S(2)}) %collective-permute-start.2) | collective-permute-done | bytes 1048608 | tf_op jit(solution)/shard_map/ppermute | solution.py:43
  59.2 22.9 %collective-permute-done.1 = f32[256,1024]{0,1:T(8,128)} collective-permute-done((f32[256,1024]{0,1:T(8,128)S(1)}, f32[256,1024]{0,1:T(8,128)}, u32[]{:S(2)}, u32[]{:S(2)}) %collective-permute-start.1) | collective-permute-done | bytes 1048608 | tf_op jit(solution)/shard_map/ppermute | solution.py:37
  85.7 5.0 gather_fusion
  90.6 5.5 copy.18
  97.4 8.1 %collective-permute-done.3 = f32[1024,1024]{1,0:T(8,128)} collective-permute-done((f32[1024,1024]{1,0:T(8,128)}, f32[1024,1024]{1,0:T(8,128)}, u32[]{:S(2)}, u32[]{:S(2)}) %collective-permute-start.3) | collective-permute-done | bytes 4194336 | tf_op jit(solution)/shard_map/ppermute | solution.py:16
  105.5 8.5 %fusion = f32[256,1024]{0,1:T(8,128)S(1)} fusion(f32[1024,1024]{1,0:T(8,128)} %collective-permute-done.3, f32[1,256,1024]{2,1,0:T(8,128)S(1)} %copy-done.1, pred[]{:T(512)S(6)} %lt.33, f32[1,256,1024]{1,2,0:T(8,128)S(1)} %copy.16), kind=kOutput, calls=%fused_computation.10 | convolution fusion | flops 3221487616 | bytes 7340033 | tf_op jit(solution)/shard_map/dot_general | solution.py:20
  117.9 12.9 %collective-permute-done.4 = f32[256,1024]{0,1:T(8,128)S(1)} collective-permute-done((f32[256,1024]{0,1:T(8,128)S(1)}, f32[256,1024]{0,1:T(8,128)S(1)}, u32[]{:S(2)}, u32[]{:S(2)}) %collective-permute-start.4) | collective-permute-done | bytes 1048608 | tf_op jit(solution)/shard_map/ppermute | solution.py:37
  130.8 9.4 %collective-permute-done.6 = f32[256,1024]{0,1:T(8,128)S(1)} collective-permute-done((f32[256,1024]{0,1:T(8,128)S(1)}, f32[256,1024]{0,1:T(8,128)S(1)}, u32[]{:S(2)}, u32[]{:S(2)}) %collective-permute-start.6) | collective-permute-done | bytes 1048608 | tf_op jit(solution)/shard_map/ppermute | solution.py:43
  140.2 13.0 %collective-permute-done.5 = f32[256,1024]{0,1:T(8,128)S(1)} collective-permute-done((f32[256,1024]{0,1:T(8,128)S(1)}, f32[256,1024]{0,1:T(8,128)S(1)}, u32[]{:S(2)}, u32[]{:S(2)}) %collective-permute-start.5) | collective-permute-done | bytes 1048608 | tf_op jit(solution)/shard_map/ppermute | solution.py:37
  155.4 4.9 gather_fusion.1
  160.4 5.4 copy.19
  167.1 165.5 %collective-permute-done.7 = f32[1024,1024]{1,0:T(8,128)} collective-permute-done((f32[1024,1024]{1,0:T(8,128)}, f32[1024,1024]{1,0:T(8,128)}, u32[]{:S(2)}, u32[]{:S(2)}) %collective-permute-start.7) | collective-permute-done | bytes 4194336 | tf_op jit(solution)/shard_map/ppermute | solution.py:16
  332.6 8.5 %convolution_select_fusion.1 = f32[256,1024]{0,1:T(8,128)S(1)} fusion(f32[256,1024]{0,1:T(8,128)S(1)} %fusion, f32[1024,1024]{1,0:T(8,128)} %collective-permute-done.7, pred[]{:T(512)S(6)} %lt.32), kind=kOutput, calls=%fused_computation.8 | convolution fusion | flops 3221487616 | bytes 6291457 | tf_op jit(solution)/shard_map/dot_general | solution.py:20
  341.2 3.8 collective-permute-start.10
  345.0 24.1 %collective-permute-done.8 = f32[256,1024]{0,1:T(8,128)S(1)} collective-permute-done((f32[256,1024]{0,1:T(8,128)S(1)}, f32[256,1024]{0,1:T(8,128)S(1)}, u32[]{:S(2)}, u32[]{:S(2)}) %collective-permute-start.8) | collective-permute-done | bytes 1048608 | tf_op jit(solution)/shard_map/ppermute | solution.py:37
  369.1 19.8 %collective-permute-done.10 = f32[256,1024]{0,1:T(8,128)S(1)} collective-permute-done((f32[256,1024]{0,1:T(8,128)S(1)}, f32[256,1024]{0,1:T(8,128)S(1)}, u32[]{:S(2)}, u32[]{:S(2)}) %collective-permute-start.10) | collective-permute-done | bytes 1048608 | tf_op jit(solution)/shard_map/ppermute | solution.py:43
  388.8 24.2 %collective-permute-done.9 = f32[256,1024]{0,1:T(8,128)S(1)} collective-permute-done((f32[256,1024]{0,1:T(8,128)S(1)}, f32[256,1024]{0,1:T(8,128)S(1)}, u32[]{:S(2)}, u32[]{:S(2)}) %collective-permute-start.9) | collective-permute-done | bytes 1048608 | tf_op jit(solution)/shard_map/ppermute | solution.py:37
  415.3 5.0 gather_fusion.2
  420.3 5.4 copy.21
  427.2 92.4 %collective-permute-done.11 = f32[1024,1024]{1,0:T(8,128)} collective-permute-done((f32[1024,1024]{1,0:T(8,128)}, f32[1024,1024]{1,0:T(8,128)}, u32[]{:S(2)}, u32[]{:S(2)}) %collective-permute-start.11) | collective-permute-done | bytes 4194336 | tf_op jit(solution)/shard_map/ppermute | solution.py:16
  519.5 8.5 %convolution_select_fusion = f32[256,1024]{0,1:T(8,128)S(1)} fusion(f32[256,1024]{0,1:T(8,128)S(1)} %convolution_select_fusion.1, f32[1024,1024]{1,0:T(8,128)} %collective-permute-done.11, pred[]{:T(512)S(6)} %lt.31), kind=kOutput, calls=%fused_computation.7 | convolution fusion | flops 3221487616 | bytes 6291457 | tf_op jit(solution)/shard_map/dot_general | solution.py:20
  531.1 5.5 fusion.5
  536.8 49.7 %all_to_all.16 = f32[256,4,512]{2,0,1:T(8,128)S(1)} all-to-all(f32[256,4,512]{2,0,1:T(8,128)S(1)} %bitcast.46), channel_id=1, replica_groups=mesh['tm'=8,'row'=4] {'row'}, dimensions={1} | all-to-all | bytes 4194304 | tf_op jit(solution)/shard_map/all_to_all | solution.py:56
  (28 shorter events, 26.8 us)
Async XLA Ops:
  7.2 520.9 %all-gather.2.cloned.1.call-start = ((), (), s32[]{:S(2)}) async-start(), calls=%async_computation.1 | async-start | bytes 1310720 | tf_op jit(solution)/shard_map/all_gather | solution.py:52
  8.8 29.2 %collective-permute-start = (f32[256,1024]{0,1:T(8,128)S(1)}, f32[256,1024]{0,1:T(8,128)S(1)}, u32[]{:S(2)}, u32[]{:S(2)}) collective-permute-start(f32[256,1024]{0,1:T(8,128)S(1)} %bitcast.41), channel_id=1, source_target_pairs={{0,1},{1,2},{2,3},{3,0},{4,5},{5,6},{6,7},{7,4},{8,9},{9,10},{10,1... | collective-permute-start | bytes 3145736 | tf_op jit(solution)/shard_map/ppermute | solution.py:37
  11.9 47.3 %collective-permute-start.2 = (f32[256,1024]{0,1:T(8,128)S(1)}, f32[256,1024]{0,1:T(8,128)S(1)}, u32[]{:S(2)}, u32[]{:S(2)}) collective-permute-start(f32[256,1024]{0,1:T(8,128)S(1)} %bitcast.42), channel_id=1, source_target_pairs={{1,0},{2,1},{3,2},{0,3},{5,4},{6,5},{7,6},{4,7},{9,8},{10,9},{11,1... | collective-permute-start | bytes 3145736 | tf_op jit(solution)/shard_map/ppermute | solution.py:43
  38.0 44.2 %collective-permute-start.1 = (f32[256,1024]{0,1:T(8,128)S(1)}, f32[256,1024]{0,1:T(8,128)}, u32[]{:S(2)}, u32[]{:S(2)}) collective-permute-start(f32[256,1024]{0,1:T(8,128)S(1)} %collective-permute-done), channel_id=1, source_target_pairs={{0,1},{1,2},{2,3},{3,0},{4,5},{5,6},{6,7},{7,4},{8,9},{9,10},{10,1... | collective-permute-start | bytes 3145736 | tf_op jit(solution)/shard_map/ppermute | solution.py:37
  90.6 14.9 %copy-start.1 = (f32[1,256,1024]{2,1,0:T(8,128)S(1)}, f32[1,256,1024]{2,1,0:T(8,128)}, u32[]{:S(2)}) copy-start(f32[1,256,1024]{2,1,0:T(8,128)} %param.3) | copy-start | bytes 3145732
  96.1 9.4 %collective-permute-start.3 = (f32[1024,1024]{1,0:T(8,128)}, f32[1024,1024]{1,0:T(8,128)}, u32[]{:S(2)}, u32[]{:S(2)}) collective-permute-start(f32[1024,1024]{1,0:T(8,128)} %bitcast.47), channel_id=1, source_target_pairs={{4,0},{8,4},{12,8},{16,12},{20,16},{24,20},{28,24},{5,1},{9,5},{13... | collective-permute-start | bytes 12582920 | tf_op jit(solution)/shard_map/ppermute | solution.py:16
  114.0 16.8 %collective-permute-start.4 = (f32[256,1024]{0,1:T(8,128)S(1)}, f32[256,1024]{0,1:T(8,128)S(1)}, u32[]{:S(2)}, u32[]{:S(2)}) collective-permute-start(f32[256,1024]{0,1:T(8,128)S(1)} %fusion), channel_id=1, source_target_pairs={{0,1},{1,2},{2,3},{3,0},{4,5},{5,6},{6,7},{7,4},{8,9},{9,10},{10,1... | collective-permute-start | bytes 3145736 | tf_op jit(solution)/shard_map/ppermute | solution.py:37
  114.1 26.1 %collective-permute-start.6 = (f32[256,1024]{0,1:T(8,128)S(1)}, f32[256,1024]{0,1:T(8,128)S(1)}, u32[]{:S(2)}, u32[]{:S(2)}) collective-permute-start(f32[256,1024]{0,1:T(8,128)S(1)} %fusion), channel_id=1, source_target_pairs={{1,0},{2,1},{3,2},{0,3},{5,4},{6,5},{7,6},{4,7},{9,8},{10,9},{11,1... | collective-permute-start | bytes 3145736 | tf_op jit(solution)/shard_map/ppermute | solution.py:43
  130.8 22.4 %collective-permute-start.5 = (f32[256,1024]{0,1:T(8,128)S(1)}, f32[256,1024]{0,1:T(8,128)S(1)}, u32[]{:S(2)}, u32[]{:S(2)}) collective-permute-start(f32[256,1024]{0,1:T(8,128)S(1)} %collective-permute-done.4), channel_id=1, source_target_pairs={{0,1},{1,2},{2,3},{3,0},{4,5},{5,6},{6,7},{7,4},{8,9},{9,10},{10,1... | collective-permute-start | bytes 3145736 | tf_op jit(solution)/shard_map/ppermute | solution.py:37
  165.8 166.8 %collective-permute-start.7 = (f32[1024,1024]{1,0:T(8,128)}, f32[1024,1024]{1,0:T(8,128)}, u32[]{:S(2)}, u32[]{:S(2)}) collective-permute-start(f32[1024,1024]{1,0:T(8,128)} %bitcast.49), channel_id=1, source_target_pairs={{8,0},{12,4},{16,8},{20,12},{24,16},{28,20},{9,1},{13,5},{17,9},{2... | collective-permute-start | bytes 12582920 | tf_op jit(solution)/shard_map/ppermute | solution.py:16
  341.1 27.9 %collective-permute-start.8 = (f32[256,1024]{0,1:T(8,128)S(1)}, f32[256,1024]{0,1:T(8,128)S(1)}, u32[]{:S(2)}, u32[]{:S(2)}) collective-permute-start(f32[256,1024]{0,1:T(8,128)S(1)} %convolution_select_fusion.1), channel_id=1, source_target_pairs={{0,1},{1,2},{2,3},{3,0},{4,5},{5,6},{6,7},{7,4},{8,9},{9,10},{10,1... | collective-permute-start | bytes 3145736 | tf_op jit(solution)/shard_map/ppermute | solution.py:37
  341.2 47.6 %collective-permute-start.10 = (f32[256,1024]{0,1:T(8,128)S(1)}, f32[256,1024]{0,1:T(8,128)S(1)}, u32[]{:S(2)}, u32[]{:S(2)}) collective-permute-start(f32[256,1024]{0,1:T(8,128)S(1)} %convolution_select_fusion.1), channel_id=1, source_target_pairs={{1,0},{2,1},{3,2},{0,3},{5,4},{6,5},{7,6},{4,7},{9,8},{10,9},{11,1... | collective-permute-start | bytes 3145736 | tf_op jit(solution)/shard_map/ppermute | solution.py:43
  369.1 44.0 %collective-permute-start.9 = (f32[256,1024]{0,1:T(8,128)S(1)}, f32[256,1024]{0,1:T(8,128)S(1)}, u32[]{:S(2)}, u32[]{:S(2)}) collective-permute-start(f32[256,1024]{0,1:T(8,128)S(1)} %collective-permute-done.8), channel_id=1, source_target_pairs={{0,1},{1,2},{2,3},{3,0},{4,5},{5,6},{6,7},{7,4},{8,9},{9,10},{10,1... | collective-permute-start | bytes 3145736 | tf_op jit(solution)/shard_map/ppermute | solution.py:37
  425.7 93.9 %collective-permute-start.11 = (f32[1024,1024]{1,0:T(8,128)}, f32[1024,1024]{1,0:T(8,128)}, u32[]{:S(2)}, u32[]{:S(2)}) collective-permute-start(f32[1024,1024]{1,0:T(8,128)} %bitcast.48), channel_id=1, source_target_pairs={{16,0},{20,4},{24,8},{28,12},{17,1},{21,5},{25,9},{29,13},{18,2},{... | collective-permute-start | bytes 12582920 | tf_op jit(solution)/shard_map/ppermute | solution.py:16
  536.6 49.9 %copy-start = (f32[256,2048]{1,0:T(8,128)}, f32[256,2048]{1,0:T(8,128)S(1)}, u32[]{:S(2)}) copy-start(f32[256,2048]{1,0:T(8,128)S(1)} %fusion.5) | copy-start | bytes 6291460
Sparse Core Ops, SparseCore 0:
  427.3 29.9 all-gather.1
